TPU v7x, 32 devices: a whole 2x2x4 slice. The times are simulated.
32 devices in a mesh: outer: 4 (over z), inner: 2 (over x), tensor: 4 (over y, core).
Axes of the slice: x: 2, y: 2, z: 4, core: 2. Of those that a mesh axis runs over, the one named last changes fastest.
Arguments:
- hidden_in: bfloat16 [16, 577, 1024], P(('outer', 'inner')), may hold values from -6 to 6
- ln1_gain: float32 [1024], replicated, may hold values from 0.5 to 1.5
- ln1_shift: float32 [1024], replicated, may hold values from -1.5 to 1.5
- w_qkv: bfloat16 [1024, 3, 1024], P(None, None, 'tensor'), may hold values from -0.1875 to 0.1875
- qkv_bias: float32 [2, 1024], P(None, 'tensor'), may hold values from -1.5 to 1.5
- w_out: bfloat16 [1024, 1024], P('tensor'), may hold values from -0.75 to 0.75
- out_bias: float32 [1024], replicated, may hold values from -1.5 to 1.5
- ln2_gain: float32 [1024], replicated, may hold values from 0.5 to 1.5
- ln2_shift: float32 [1024], replicated, may hold values from -1.5 to 1.5
- w_fc1: bfloat16 [1024, 4096], P(None, 'tensor'), may hold values from -0.1875 to 0.1875
- fc1_bias: float32 [4096], P('tensor'), may hold values from -1.5 to 1.5
- w_fc2: bfloat16 [4096, 1024], P('tensor'), may hold values from -0.09375 to 0.09375
- fc2_bias: float32 [1024], replicated, may hold values from -1.5 to 1.5
- flags: int32 [16], P(('outer', 'inner')), may hold values 0 or 1
- out_grad: bfloat16 [16, 577, 1024], P(('outer', 'inner')), may hold values from -6 to 6
Outputs:
- block_out: bfloat16 [16, 577, 1024], P(('outer', 'inner'))
- in_grad: bfloat16 [16, 577, 1024], P(('outer', 'inner'))
- g_ln1_gain: float32 [1024], replicated
- g_ln1_shift: float32 [1024], replicated
- g_w_qkv: float32 [1024, 3, 1024], P(None, None, 'tensor')
- g_qkv_bias: float32 [2, 1024], P(None, 'tensor')
- g_w_out: float32 [1024, 1024], P('tensor')
- g_out_bias: float32 [1024], replicated
- g_ln2_gain: float32 [1024], replicated
- g_ln2_shift: float32 [1024], replicated
- g_w_fc1: float32 [1024, 4096], P(None, 'tensor')
- g_fc1_bias: float32 [4096], P('tensor')
- g_w_fc2: float32 [4096, 1024], P('tensor')
- g_fc2_bias: float32 [1024], replicated
Inputs may be any that keep to these rules, and one draw needn't show every extreme that they name: `flags`: 1 marks an image, 0 a padded slot.
All inputs are finite; a program needn't handle non-finite values. No bound on the sum of `flags` on one device may be relied on, other than what follows from the above.
Results may differ from a plain program's by a relative error of at most 0.012.
Values sent between devices are 32-bit elements; how exact they have to be, the bound alone decides.
No kernel may reach another device: no remote copies, remote signals or barrier semaphores. Data moves between devices by JAX's collectives and lax.ppermute only.
A program may use at most 192 MiB of HBM per device.

v0:
```python
import jax
import jax.numpy as jnp
from jax import lax
from jax.sharding import PartitionSpec as P

HD = 64


norm_eps = 1e-05


def layer_norm(values_in, gain_vec, shift_vec):
    row_mean = jnp.mean(values_in, axis=-1, keepdims=True)
    centered = values_in - row_mean
    row_var = jnp.mean(centered * centered, axis=-1, keepdims=True)
    return centered * lax.rsqrt(row_var + norm_eps) * gain_vec + shift_vec


def quick_gelu(values_in):
    return values_in * jax.nn.sigmoid(1.702 * values_in)


def gelu_slope(values_in):
    sig_val = jax.nn.sigmoid(1.702 * values_in)
    return sig_val + 1.702 * values_in * sig_val * (1.0 - sig_val)


def mat_prod(left, right):
    return jnp.dot(left, right, preferred_element_type=jnp.float32)


def left_contract(left, right):
    return lax.dot_general(
        left, right, (((0,), (0,)), ((), ())), preferred_element_type=jnp.float32
    )


def right_contract(left, right):
    return lax.dot_general(
        left, right, (((1,), (1,)), ((), ())), preferred_element_type=jnp.float32
    )


def col_sum(values_in):
    return jnp.sum(values_in.astype(jnp.float32), axis=0)


def attn_scores(q_heads, k_heads, score_scale):
    return (
        jnp.einsum("bqhd,bkhd->bhqk", q_heads, k_heads, preferred_element_type=jnp.float32)
        * score_scale
    )


def per_device(
    hidden_in,
    ln1_gain,
    ln1_shift,
    w_qkv,
    qkv_bias,
    w_out,
    out_bias,
    ln2_gain,
    ln2_shift,
    w_fc1,
    fc1_bias,
    w_fc2,
    fc2_bias,
    flags,
    out_grad,
):
    img_count, seq_len, model_width = hidden_in.shape
    row_count = img_count * seq_len
    head_cols = w_qkv.shape[2]
    head_count = head_cols // HD
    score_scale = HD ** (-0.5)
    head_shape = (img_count, seq_len, head_count, HD)
    qkv_flat = w_qkv.reshape(model_width, 3 * head_cols)
    x_rows = hidden_in.reshape(row_count, model_width).astype(jnp.float32)
    normed1 = layer_norm(x_rows, ln1_gain, ln1_shift).astype(jnp.bfloat16)
    projected = mat_prod(normed1, qkv_flat).reshape(row_count, 3, head_cols)
    q_heads = (projected[:, 0] + qkv_bias[0]).astype(jnp.bfloat16).reshape(head_shape)
    k_heads = projected[:, 1].astype(jnp.bfloat16).reshape(head_shape)
    v_heads = (projected[:, 2] + qkv_bias[1]).astype(jnp.bfloat16).reshape(head_shape)
    scores = attn_scores(q_heads, k_heads, score_scale)
    log_total = jax.nn.logsumexp(scores, axis=-1, keepdims=True)
    attn_probs = jnp.exp(scores - log_total).astype(jnp.bfloat16)
    attended = jnp.einsum(
        "bhqk,bkhd->bqhd", attn_probs, v_heads, preferred_element_type=jnp.float32
    )
    attended = attended.astype(jnp.bfloat16).reshape(row_count, head_cols)
    attn_total = lax.psum(mat_prod(attended, w_out), "tensor")
    resid_mid = x_rows + attn_total + out_bias
    normed2 = layer_norm(resid_mid, ln2_gain, ln2_shift).astype(jnp.bfloat16)
    pre_act = mat_prod(normed2, w_fc1) + fc1_bias
    gelu_out = quick_gelu(pre_act).astype(jnp.bfloat16)
    mlp_total = lax.psum(mat_prod(gelu_out, w_fc2), "tensor")
    block_out = (resid_mid + mlp_total + fc2_bias).astype(jnp.bfloat16).reshape(hidden_in.shape)
    out_cot = (out_grad.astype(jnp.float32) * flags.astype(jnp.float32)[:, None, None]).reshape(
        row_count, model_width
    )
    g_fc2_bias = jnp.sum(out_cot, axis=0)
    mlp_cot = out_cot.astype(jnp.bfloat16)
    g_w_fc2 = left_contract(gelu_out, mlp_cot)
    pre_grad = (right_contract(mlp_cot, w_fc2) * gelu_slope(pre_act)).astype(jnp.bfloat16)
    g_w_fc1 = left_contract(normed2, pre_grad)
    g_fc1_bias = col_sum(pre_grad)
    norm2_grad = lax.psum(right_contract(pre_grad, w_fc1), "tensor")
    unused_two, norm2_pull = jax.vjp(layer_norm, resid_mid, ln2_gain, ln2_shift)
    mid_from_norm, g_ln2_gain, g_ln2_shift = norm2_pull(norm2_grad)
    resid_grad = out_cot + mid_from_norm
    g_out_bias = jnp.sum(resid_grad, axis=0)
    attn_cot = resid_grad.astype(jnp.bfloat16)
    g_w_out = left_contract(attended, attn_cot)
    attended_grad = right_contract(attn_cot, w_out).astype(jnp.bfloat16).reshape(head_shape)
    again = attn_scores(q_heads, k_heads, score_scale)
    probs_again = jnp.exp(again - log_total)
    probs_low = probs_again.astype(jnp.bfloat16)
    probs_grad = jnp.einsum(
        "bqhd,bkhd->bhqk", attended_grad, v_heads, preferred_element_type=jnp.float32
    )
    row_dot = jnp.sum(probs_again * probs_grad, axis=-1, keepdims=True)
    score_grad = (probs_again * (probs_grad - row_dot)).astype(jnp.bfloat16)
    q_grad = (
        jnp.einsum("bhqk,bkhd->bqhd", score_grad, k_heads, preferred_element_type=jnp.float32)
        * score_scale
    ).astype(jnp.bfloat16)
    k_grad = (
        jnp.einsum("bhqk,bqhd->bkhd", score_grad, q_heads, preferred_element_type=jnp.float32)
        * score_scale
    ).astype(jnp.bfloat16)
    v_grad = jnp.einsum(
        "bhqk,bqhd->bkhd", probs_low, attended_grad, preferred_element_type=jnp.float32
    ).astype(jnp.bfloat16)
    q_rows = q_grad.reshape(row_count, head_cols)
    v_rows = v_grad.reshape(row_count, head_cols)
    qkv_grad = jnp.stack([q_rows, k_grad.reshape(row_count, head_cols), v_rows], axis=1).reshape(
        row_count, 3 * head_cols
    )
    g_w_qkv = left_contract(normed1, qkv_grad).reshape(model_width, 3, head_cols)
    g_qkv_bias = jnp.stack([col_sum(q_rows), col_sum(v_rows)], axis=0)
    norm1_grad = lax.psum(right_contract(qkv_grad, qkv_flat), "tensor")
    unused_one, norm1_pull = jax.vjp(layer_norm, x_rows, ln1_gain, ln1_shift)
    x_from_norm, g_ln1_gain, g_ln1_shift = norm1_pull(norm1_grad)
    in_grad = (resid_grad + x_from_norm).astype(jnp.bfloat16).reshape(hidden_in.shape)
    shares = (
        lax.psum_scatter(g_ln1_gain, "inner", scatter_dimension=0, tiled=True),
        lax.psum_scatter(g_ln1_shift, "inner", scatter_dimension=0, tiled=True),
        lax.psum_scatter(g_w_qkv, "inner", scatter_dimension=0, tiled=True),
        lax.psum_scatter(g_qkv_bias, "inner", scatter_dimension=1, tiled=True),
        lax.psum_scatter(g_w_out, "inner", scatter_dimension=1, tiled=True),
        lax.psum_scatter(g_out_bias, "inner", scatter_dimension=0, tiled=True),
        lax.psum_scatter(g_ln2_gain, "inner", scatter_dimension=0, tiled=True),
        lax.psum_scatter(g_ln2_shift, "inner", scatter_dimension=0, tiled=True),
        lax.psum_scatter(g_w_fc1, "inner", scatter_dimension=0, tiled=True),
        lax.psum_scatter(g_fc1_bias, "inner", scatter_dimension=0, tiled=True),
        lax.psum_scatter(g_w_fc2, "inner", scatter_dimension=1, tiled=True),
        lax.psum_scatter(g_fc2_bias, "inner", scatter_dimension=0, tiled=True),
    )
    shares = lax.psum(
        (
            shares[0],
            shares[1],
            shares[2],
            shares[3],
            shares[4],
            shares[5],
            shares[6],
            shares[7],
            shares[8],
            shares[9],
            shares[10],
            shares[11],
        ),
        "outer",
    )
    (
        s_ln1_gain,
        s_ln1_shift,
        s_w_qkv,
        s_qkv_bias,
        s_w_out,
        s_out_bias,
        s_ln2_gain,
        s_ln2_shift,
        s_w_fc1,
        s_fc1_bias,
        s_w_fc2,
        s_fc2_bias,
    ) = shares
    summed = (
        lax.all_gather(s_ln1_gain, "inner", axis=0, tiled=True),
        lax.all_gather(s_ln1_shift, "inner", axis=0, tiled=True),
        lax.all_gather(s_w_qkv, "inner", axis=0, tiled=True),
        lax.all_gather(s_qkv_bias, "inner", axis=1, tiled=True),
        lax.all_gather(s_w_out, "inner", axis=1, tiled=True),
        lax.all_gather(s_out_bias, "inner", axis=0, tiled=True),
        lax.all_gather(s_ln2_gain, "inner", axis=0, tiled=True),
        lax.all_gather(s_ln2_shift, "inner", axis=0, tiled=True),
        lax.all_gather(s_w_fc1, "inner", axis=0, tiled=True),
        lax.all_gather(s_fc1_bias, "inner", axis=0, tiled=True),
        lax.all_gather(s_w_fc2, "inner", axis=1, tiled=True),
        lax.all_gather(s_fc2_bias, "inner", axis=0, tiled=True),
    )
    return (
        block_out,
        in_grad,
        summed[0],
        summed[1],
        summed[2],
        summed[3],
        summed[4],
        summed[5],
        summed[6],
        summed[7],
        summed[8],
        summed[9],
        summed[10],
        summed[11],
    )


def solution(mesh):
    placed = (
        P(("outer", "inner"), None, None),
        P(),
        P(),
        P(None, None, "tensor"),
        P(None, "tensor"),
        P("tensor", None),
        P(),
        P(),
        P(),
        P(None, "tensor"),
        P("tensor"),
        P("tensor", None),
        P(),
        P(("outer", "inner")),
        P(("outer", "inner"), None, None),
    )
    return jax.shard_map(
        per_device,
        mesh=mesh,
        in_specs=placed,
        out_specs=(
            P(("outer", "inner"), None, None),
            P(("outer", "inner"), None, None),
            P(),
            P(),
            P(None, None, "tensor"),
            P(None, "tensor"),
            P("tensor", None),
            P(),
            P(),
            P(),
            P(None, "tensor"),
            P("tensor"),
            P("tensor", None),
            P(),
        ),
        check_vma=False,
    )
```

profile of v0, /device:TPU:0, one launch (start us, length us, event | category | flops | bytes accessed | tf_op | source)
XLA Modules:
  0.0 1097.7 jit_solution(336543928301203086)
XLA Ops:
  18.4 5.7 add_convert_fusion.3
  71.4 4.8 copy.109
  83.6 4.9 reshape.226
  88.6 5.1 reshape.230
  93.6 74.8 %all-reduce.16.cloned.1.call-done = f32[1154,1024]{1,0:T(8,128)} async-done(((f32[1154,1024]{1,0:T(8,128)}), f32[1154,1024]{1,0:T(8,128)}) %all-reduce.16.cloned.1.call-update) | async-done | bytes 4726800 | tf_op jit(solution)/shard_map/psum | solution.py:92
  179.3 4.7 convert_reduce_fusion
  189.8 94.8 %all-reduce.18.cloned.1.call-done = f32[1154,1024]{1,0:T(8,128)} async-done(((f32[1154,1024]{1,0:T(8,128)}), f32[1154,1024]{1,0:T(8,128)}) %all-reduce.18.cloned.1.call-update) | async-done | bytes 4726800 | tf_op jit(solution)/shard_map/psum | solution.py:108
  284.7 5.4 multiply_reduce_fusion.2
  298.8 8.5 fusion.26
  307.4 8.8 fusion.15
  325.9 8.4 convert_reduce_fusion.2
  339.7 8.0 multiply_reduce_fusion
  347.7 6.6 multiply_convert_fusion
  363.4 4.8 convert_reduce_fusion.3
  376.1 5.7 fusion.2
  381.9 51.8 %reduce-scatter.14.cloned.1.call-done = f32[1024,512]{1,0:T(8,128)} async-done(((f32[1024,1024]{1,0:T(8,128)}), f32[1024,512]{1,0:T(8,128)}) %reduce-scatter.14.cloned.1.call-update) | async-done | bytes 2097168 | tf_op jit(solution)/shard_map/reduce_scatter | solution.py:157
  433.7 46.1 %reduce-scatter.8.cloned.1.call-done = f32[512,3,256]{2,0,1:T(8,128)} async-done(((f32[1024,3,256]{2,0,1:T(8,128)}), f32[512,3,256]{2,0,1:T(8,128)}) %reduce-scatter.8.cloned.1.call-update) | async-done | bytes 1572880 | tf_op jit(solution)/shard_map/reduce_scatter | solution.py:149
  479.9 6.7 fusion.27
  487.7 6.8 convolution_bitcast_fusion
  494.7 210.8 %all-reduce.22.cloned.1.call-done = (f32[512,3,256]{2,0,1:T(8,128)}, f32[256,512]{1,0:T(8,128)}, f32[512,1024]{1,0:T(8,128)}, f32[1024,512]{1,0:T(8,128)}) async-done(((f32[512,3,256]{2,0,1:T(8,128)}, f32[256,512]{1,0:T(8,128)}, f32[512,1024]{1,0:T(8,128)}, f32[1024,512]{1,0:T(8,128)}), (f32[512,3,256]{2,0,1:T(8,128)}, f32[256,512]{1,0:T(8,128)}, f32[512,1024]{1,0:T(8,128)}, ...) | async-done | bytes 6291472 | tf_op jit(solution)/shard_map/psum | solution.py:160
  709.1 8.4 reduce-scatter.16.cloned.1.call-done
  718.4 172.7 %all-reduce.20.cloned.1.call-done = (f32[1154,1024]{1,0:T(8,128)}, f32[1154,1024]{1,0:T(8,128)}) async-done(((f32[1154,1024]{1,0:T(8,128)}, f32[1154,1024]{1,0:T(8,128)}), (f32[1154,1024]{1,0:T(8,128)}, f32[1154,1024]{1,0:T(8,128)})) %all-reduce.20.cloned.1.call-update) | async-done | bytes 9453584 | tf_op jit(solution)/shard_map/psum | solution.py:97
  891.1 6.5 add_convert_fusion.1
  901.2 5.7 copy.140
  911.2 8.3 all-reduce.10
  920.1 18.8 %all-reduce.8 = (f32[512]{0:T(512)S(1)}, f32[512]{0:T(512)S(1)}, f32[2,128]{1,0:T(2,128)S(1)}, f32[512]{0:T(512)S(1)}, f32[512]{0:T(512)S(1)}, /*index=5*/f32[512]{0:T(512)S(1)}, f32[512]{0:T(512)S(1)}, f32[512]{0:T(512)S(1)}) all-reduce(f32[512]{0:T(512)S(1)} %dynamic-slice.1, ...), channel_id=1, replica_groups=mesh['outer'=4,'inner'=2,'tensor'=4] {'outer'}, use_global_device_ids=true, to_apply=%region_17.0 | all-reduce | flops 3840 | bytes 30720 | tf_op jit(solution)/shard_map/psum | solution.py:160
  938.9 4.5 all-gather.1
  969.9 4.7 all-gather.6
  974.6 5.0 fusion.30
  985.1 5.5 copy.141
  990.6 28.2 %all-gather.16.cloned.1.call-done = f32[1024,1024]{1,0:T(8,128)} async-done(((f32[512,1024]{1,0:T(8,128)}), f32[1024,1024]{1,0:T(8,128)}) %all-gather.16.cloned.1.call-update) | async-done | bytes 4194320 | tf_op jit(solution)/shard_map/all_gather | solution.py:200
  1018.8 58.3 %all-gather.18.cloned.1.call-done = f32[1024,1024]{1,0:T(8,128)} async-done(((f32[1024,512]{1,0:T(8,128)}), f32[1024,1024]{1,0:T(8,128)}) %all-gather.18.cloned.1.call-update) | async-done | bytes 4194320 | tf_op jit(solution)/shard_map/all_gather | solution.py:202
  (208 shorter events, 182.1 us)
Async XLA Ops:
  7.2 172.0 %copy-start = (bf16[1024,1024]{1,0:T(8,128)(2,1)S(1)}, bf16[1024,1024]{1,0:T(8,128)(2,1)}, u32[]{:S(2)}) copy-start(bf16[1024,1024]{1,0:T(8,128)(2,1)} %param.26) | copy-start | bytes 6291460
  7.2 11.2 %copy-start.18 = (f32[1024]{0:T(1024)S(1)}, f32[1024]{0:T(1024)}, u32[]{:S(2)}) copy-start(f32[1024]{0:T(1024)} %param.16) | copy-start | bytes 12292
  7.2 11.2 %copy-start.24 = (f32[1024]{0:T(1024)S(1)}, f32[1024]{0:T(1024)}, u32[]{:S(2)}) copy-start(f32[1024]{0:T(1024)} %param.17) | copy-start | bytes 12292
  7.2 161.3 %all-reduce.16.cloned.1.call-start = ((), (), s32[]{:S(2)}) async-start(), calls=%async_computation.5 | async-start | bytes 9502720 | tf_op jit(solution)/shard_map/psum | solution.py:92
  11.0 13.0 %copy-start.11 = (f32[2,577]{0,1:T(8,128)}, f32[2,577]{0,1:T(8,128)S(1)}, u32[]{:S(2)}) copy-start(f32[2,577]{0,1:T(8,128)S(1)} %broadcast_multiply_fusion) | copy-start | bytes 13852
  71.1 213.6 %all-reduce.18.cloned.1.call-start = ((), (), s32[]{:S(2)}) async-start(), calls=%async_computation.6 | async-start | bytes 9502720 | tf_op jit(solution)/shard_map/psum | solution.py:108
  88.6 79.9 %copy-start.22 = (f32[1024]{0:T(1024)S(1)}, f32[1024]{0:T(1024)}, u32[]{:S(2)}) copy-start(f32[1024]{0:T(1024)} %param.21) | copy-start | bytes 12292
  172.9 6.3 copy-start.2
  172.9 6.3 slice-start.2
  189.8 192.1 %reduce-scatter.10.cloned.1.call-start = ((), (), s32[]{:S(2)}) async-start(), calls=%async_computation.9 | async-start | bytes 1572864 | tf_op jit(solution)/shard_map/reduce_scatter | solution.py:151
  284.7 9.4 slice-start.4
  298.8 83.2 %reduce-scatter.12.cloned.1.call-start = ((), (), s32[]{:S(2)}) async-start(), calls=%async_computation.11 | async-start | bytes 6291456 | tf_op jit(solution)/shard_map/reduce_scatter | solution.py:155
  307.3 126.4 %reduce-scatter.14.cloned.1.call-start = ((), (), s32[]{:S(2)}) async-start(), calls=%async_computation.13 | async-start | bytes 6291456 | tf_op jit(solution)/shard_map/reduce_scatter | solution.py:157
  316.2 163.6 %reduce-scatter.8.cloned.1.call-start = ((), (), s32[]{:S(2)}) async-start(), calls=%async_computation.7 | async-start | bytes 4718592 | tf_op jit(solution)/shard_map/reduce_scatter | solution.py:149
  347.7 9.2 copy-start.8
  356.9 6.5 copy-start.10
  381.8 323.6 %all-reduce.22.cloned.1.call-start = ((), (), s32[]{:S(2)}) async-start(), calls=%async_computation.17 | async-start | bytes 12582912 | tf_op jit(solution)/shard_map/psum | solution.py:160
  479.9 237.6 %reduce-scatter.16.cloned.1.call-start = ((), (), s32[]{:S(2)}) async-start(), calls=%async_computation.15 | async-start | bytes 196608
  487.6 403.4 %all-reduce.20.cloned.1.call-start = ((), (), s32[]{:S(2)}) async-start(), calls=%async_computation.16 | async-start | bytes 19005440 | tf_op jit(solution)/shard_map/psum | solution.py:97
  494.6 213.0 %copy-start.12 = (f32[2,577]{0,1:T(8,128)S(1)}, f32[2,577]{0,1:T(8,128)}, u32[]{:S(2)}) copy-start(f32[2,577]{0,1:T(8,128)} %copy-done.11) | copy-start | bytes 13852
  494.6 213.2 %copy-start.20 = (f32[2,577]{1,0:T(2,128)S(1)}, f32[2,577]{1,0:T(2,128)}, u32[]{:S(2)}) copy-start(f32[2,577]{1,0:T(2,128)} %get-tuple-element.111) | copy-start | bytes 13852
  494.6 213.3 %copy-start.30 = (u32[32]{0:T(128)S(1)}, u32[32]{0:T(128)}, u32[]{:S(2)}) copy-start(u32[32]{0:T(128)} %constant.32) | copy-start | bytes 388
  494.6 396.5 %copy-start.23 = (f32[1024]{0:T(1024)S(1)}, f32[1024]{0:T(1024)}, u32[]{:S(2)}) copy-start(f32[1024]{0:T(1024)} %param.27) | copy-start | bytes 12292
  494.6 496.0 %all-gather.14.cloned.1.call-start = ((), (), s32[]{:S(2)}) async-start(), calls=%async_computation.10 | async-start | bytes 1572864 | tf_op jit(solution)/shard_map/all_gather | solution.py:196
  705.4 285.2 %all-gather.12.cloned.1.call-start = ((), (), s32[]{:S(2)}) async-start(), calls=%async_computation.8 | async-start | bytes 4718592 | tf_op jit(solution)/shard_map/all_gather | solution.py:194
  706.2 312.7 %all-gather.16.cloned.1.call-start = ((), (), s32[]{:S(2)}) async-start(), calls=%async_computation.12 | async-start | bytes 6291456 | tf_op jit(solution)/shard_map/all_gather | solution.py:200
  706.8 370.4 %all-gather.18.cloned.1.call-start = ((), (), s32[]{:S(2)}) async-start(), calls=%async_computation.14 | async-start | bytes 6291456 | tf_op jit(solution)/shard_map/all_gather | solution.py:202
  897.5 9.4 copy-start.19
  901.2 5.7 copy-start.6
  906.9 72.7 %slice-start = ((s8[4751360]{0:T(1024)(128)(4,1)}), s8[557056]{0:T(1024)(128)(4,1)S(1)}, s32[]{:S(2)}) async-start(s8[4751360]{0:T(1024)(128)(4,1)} %bitcast.68), calls=%async_computation.18 | async-start | bytes 1114112
  990.6 92.1 %copy-start.16 = (f32[256,1024]{1,0:T(8,128)S(1)}, f32[256,1024]{1,0:T(8,128)}, u32[]{:S(2)}) copy-start(f32[256,1024]{1,0:T(8,128)} %all-gather.14.cloned.1.call-done) | copy-start | bytes 3145732
  1077.1 8.4 copy-start.13
  (20 other events, 68.3 us)
Sparse Core Ops, SparseCore 0:
  71.2 97.2 all-reduce.15
  189.9 94.6 all-reduce.17
  298.9 20.5 reduce-scatter.9
  322.2 54.3 reduce-scatter.11
  379.3 54.3 reduce-scatter.13
  436.4 43.3 reduce-scatter.7
  482.5 222.9 all-reduce.21
  708.2 9.2 reduce-scatter.15
  720.1 170.9 all-reduce.19
  892.5 21.4 all-gather.13
  915.5 45.1 all-gather.11
  962.0 56.7 all-gather.15
  1020.4 56.6 all-gather.17
where the time goes:
time: 1100 us
  waiting for transfers between devices  748 us (68%)
  local copies, waits for them, and re-layouts  120 us (11%)
  matrix products  92.2 us (8%)
  blocking collectives  62.9 us (6%)
  other arithmetic  58.5 us (5%)
  between operations  15.7 us (1%)
    psum x1, waiting for transfers between devices, per_device(): lax.psum((shares[0], shares[1], shares[2], shares[3], shares[4], shares[5...  211 us
    psum x1, waiting for transfers between devices, per_device(): mlp_total = lax.psum(mat_prod(gelu_out, w_fc2), 'tensor')  173 us
    psum x1, waiting for transfers between devices, per_device(): norm2_grad = lax.psum(right_contract(pre_grad, w_fc1), 'tensor')  94.8 us
    psum x1, waiting for transfers between devices, per_device(): attn_total = lax.psum(mat_prod(attended, w_out), 'tensor')  74.8 us
    all_gather x1, waiting for transfers between devices, per_device(): lax.all_gather(s_w_fc2, 'inner', axis=1, tiled=True)  58.3 us
    reduce_scatter x1, waiting for transfers between devices, per_device(): lax.psum_scatter(g_w_fc2, 'inner', scatter_dimension=1, tiled=True)  51.8 us
    reduce_scatter x1, waiting for transfers between devices, per_device(): lax.psum_scatter(g_w_qkv, 'inner', scatter_dimension=0, tiled=True)  46.1 us
    unnamed x106, local copies, waits for them, and re-layouts  45.4 us
  transfers between devices with their start and end apart: 13, of which 9 were waited for; matrix products, arithmetic and copies ran while one was open for 14% of the time, Pallas kernels for 0%

commit v1 on v0

--- a/solution.py
+++ b/solution.py
@@ -1,3 +1,5 @@
+import functools
+
 import jax
 import jax.numpy as jnp
 from jax import lax
@@ -52,7 +54,34 @@
     )
 
 
+def tensor_sum(make, width, n_tensor):
+    if n_tensor == 1:
+        return make(0, width)
+    if n_tensor == 2:
+        part = make(0, width)
+        return part + lax.ppermute(part, "tensor", [(i, i ^ 1) for i in range(2)])
+    if n_tensor != 4 or width % 256:
+        return lax.psum(make(0, width), "tensor")
+    low_bit = lax.axis_index("tensor") % 2
+    half = width // 2
+    keep = make(low_bit * half, half)
+    send = make((1 - low_bit) * half, half)
+    near = [(i, i ^ 1) for i in range(4)]
+    far = [(i, i ^ 2) for i in range(4)]
+    part = keep + lax.ppermute(send, "tensor", near)
+    total = part + lax.ppermute(part, "tensor", far)
+    back = lax.ppermute(total, "tensor", near)
+    first = jnp.where(low_bit == 0, total, back)
+    second = jnp.where(low_bit == 0, back, total)
+    return jnp.concatenate([first, second], axis=1)
+
+
+def cols(weight, start, size, axis):
+    return lax.dynamic_slice_in_dim(weight, start, size, axis)
+
+
 def per_device(
+    n_tensor,
     hidden_in,
     ln1_gain,
     ln1_shift,
@@ -89,12 +118,16 @@
         "bhqk,bkhd->bqhd", attn_probs, v_heads, preferred_element_type=jnp.float32
     )
     attended = attended.astype(jnp.bfloat16).reshape(row_count, head_cols)
-    attn_total = lax.psum(mat_prod(attended, w_out), "tensor")
+    attn_total = tensor_sum(
+        lambda s, w: mat_prod(attended, cols(w_out, s, w, 1)), model_width, n_tensor
+    )
     resid_mid = x_rows + attn_total + out_bias
     normed2 = layer_norm(resid_mid, ln2_gain, ln2_shift).astype(jnp.bfloat16)
     pre_act = mat_prod(normed2, w_fc1) + fc1_bias
     gelu_out = quick_gelu(pre_act).astype(jnp.bfloat16)
-    mlp_total = lax.psum(mat_prod(gelu_out, w_fc2), "tensor")
+    mlp_total = tensor_sum(
+        lambda s, w: mat_prod(gelu_out, cols(w_fc2, s, w, 1)), model_width, n_tensor
+    )
     block_out = (resid_mid + mlp_total + fc2_bias).astype(jnp.bfloat16).reshape(hidden_in.shape)
     out_cot = (out_grad.astype(jnp.float32) * flags.astype(jnp.float32)[:, None, None]).reshape(
         row_count, model_width
@@ -105,7 +138,9 @@
     pre_grad = (right_contract(mlp_cot, w_fc2) * gelu_slope(pre_act)).astype(jnp.bfloat16)
     g_w_fc1 = left_contract(normed2, pre_grad)
     g_fc1_bias = col_sum(pre_grad)
-    norm2_grad = lax.psum(right_contract(pre_grad, w_fc1), "tensor")
+    norm2_grad = tensor_sum(
+        lambda s, w: right_contract(pre_grad, cols(w_fc1, s, w, 0)), model_width, n_tensor
+    )
     unused_two, norm2_pull = jax.vjp(layer_norm, resid_mid, ln2_gain, ln2_shift)
     mid_from_norm, g_ln2_gain, g_ln2_shift = norm2_pull(norm2_grad)
     resid_grad = out_cot + mid_from_norm
@@ -139,84 +174,57 @@
     )
     g_w_qkv = left_contract(normed1, qkv_grad).reshape(model_width, 3, head_cols)
     g_qkv_bias = jnp.stack([col_sum(q_rows), col_sum(v_rows)], axis=0)
-    norm1_grad = lax.psum(right_contract(qkv_grad, qkv_flat), "tensor")
+    norm1_grad = tensor_sum(
+        lambda s, w: right_contract(qkv_grad, cols(qkv_flat, s, w, 0)), model_width, n_tensor
+    )
     unused_one, norm1_pull = jax.vjp(layer_norm, x_rows, ln1_gain, ln1_shift)
     x_from_norm, g_ln1_gain, g_ln1_shift = norm1_pull(norm1_grad)
     in_grad = (resid_grad + x_from_norm).astype(jnp.bfloat16).reshape(hidden_in.shape)
-    shares = (
-        lax.psum_scatter(g_ln1_gain, "inner", scatter_dimension=0, tiled=True),
-        lax.psum_scatter(g_ln1_shift, "inner", scatter_dimension=0, tiled=True),
-        lax.psum_scatter(g_w_qkv, "inner", scatter_dimension=0, tiled=True),
-        lax.psum_scatter(g_qkv_bias, "inner", scatter_dimension=1, tiled=True),
-        lax.psum_scatter(g_w_out, "inner", scatter_dimension=1, tiled=True),
-        lax.psum_scatter(g_out_bias, "inner", scatter_dimension=0, tiled=True),
-        lax.psum_scatter(g_ln2_gain, "inner", scatter_dimension=0, tiled=True),
-        lax.psum_scatter(g_ln2_shift, "inner", scatter_dimension=0, tiled=True),
-        lax.psum_scatter(g_w_fc1, "inner", scatter_dimension=0, tiled=True),
-        lax.psum_scatter(g_fc1_bias, "inner", scatter_dimension=0, tiled=True),
-        lax.psum_scatter(g_w_fc2, "inner", scatter_dimension=1, tiled=True),
-        lax.psum_scatter(g_fc2_bias, "inner", scatter_dimension=0, tiled=True),
-    )
-    shares = lax.psum(
-        (
-            shares[0],
-            shares[1],
-            shares[2],
-            shares[3],
-            shares[4],
-            shares[5],
-            shares[6],
-            shares[7],
-            shares[8],
-            shares[9],
-            shares[10],
-            shares[11],
-        ),
-        "outer",
-    )
-    (
-        s_ln1_gain,
-        s_ln1_shift,
-        s_w_qkv,
-        s_qkv_bias,
-        s_w_out,
-        s_out_bias,
-        s_ln2_gain,
-        s_ln2_shift,
-        s_w_fc1,
-        s_fc1_bias,
-        s_w_fc2,
-        s_fc2_bias,
-    ) = shares
-    summed = (
-        lax.all_gather(s_ln1_gain, "inner", axis=0, tiled=True),
-        lax.all_gather(s_ln1_shift, "inner", axis=0, tiled=True),
-        lax.all_gather(s_w_qkv, "inner", axis=0, tiled=True),
-        lax.all_gather(s_qkv_bias, "inner", axis=1, tiled=True),
-        lax.all_gather(s_w_out, "inner", axis=1, tiled=True),
-        lax.all_gather(s_out_bias, "inner", axis=0, tiled=True),
-        lax.all_gather(s_ln2_gain, "inner", axis=0, tiled=True),
-        lax.all_gather(s_ln2_shift, "inner", axis=0, tiled=True),
-        lax.all_gather(s_w_fc1, "inner", axis=0, tiled=True),
-        lax.all_gather(s_fc1_bias, "inner", axis=0, tiled=True),
-        lax.all_gather(s_w_fc2, "inner", axis=1, tiled=True),
-        lax.all_gather(s_fc2_bias, "inner", axis=0, tiled=True),
+    small = jnp.concatenate(
+        [
+            g_ln1_gain,
+            g_ln1_shift,
+            g_qkv_bias.reshape(-1),
+            g_out_bias,
+            g_ln2_gain,
+            g_ln2_shift,
+            g_fc1_bias,
+            g_fc2_bias,
+        ]
+    )
+    small = lax.psum(small, ("outer", "inner"))
+    cuts = [model_width] * 2 + [g_qkv_bias.size] + [model_width] * 3
+    cuts += [g_fc1_bias.size, model_width]
+    pieces = []
+    offset = 0
+    for size in cuts:
+        pieces.append(small[offset : offset + size])
+        offset += size
+    big = (g_w_qkv, g_w_out, g_w_fc1, g_w_fc2)
+    big_dims = (0, 1, 0, 1)
+    shares = tuple(
+        lax.psum_scatter(g, "inner", scatter_dimension=d, tiled=True)
+        for g, d in zip(big, big_dims)
+    )
+    shares = lax.psum(shares, "outer")
+    summed = tuple(
+        lax.all_gather(s, "inner", axis=d, tiled=True) for s, d in zip(shares, big_dims)
     )
     return (
         block_out,
         in_grad,
+        pieces[0],
+        pieces[1],
         summed[0],
+        pieces[2].reshape(g_qkv_bias.shape),
         summed[1],
+        pieces[3],
+        pieces[4],
+        pieces[5],
         summed[2],
+        pieces[6],
         summed[3],
-        summed[4],
-        summed[5],
-        summed[6],
-        summed[7],
-        summed[8],
-        summed[9],
-        summed[10],
-        summed[11],
+        pieces[7],
     )
 
 
@@ -239,7 +247,7 @@
         P(("outer", "inner"), None, None),
     )
     return jax.shard_map(
-        per_device,
+        functools.partial(per_device, mesh.shape["tensor"]),
         mesh=mesh,
         in_specs=placed,
         out_specs=(

time: 1100 us -> 898 us (0.82)
  waiting for transfers between devices: 748 us -> 521 us
  other arithmetic: 58.5 us -> 99.2 us
  blocking collectives: 62.9 us -> 35.8 us
    psum x4 -> x1, waiting for transfers between devices: 553 us -> 225 us  [per_device(): shares = lax.psum(shares, 'outer')]
    ppermute x0 -> x12, waiting for transfers between devices: none -> 208 us  [the longest x4 196 us: tensor_sum(): total = part + lax.ppermute(part, 'tensor', far)]
    reduce_scatter x4, waiting for transfers between devices: 97.9 us -> 49 us  [per_device(): lax.psum_scatter(g, 'inner', scatter_dimension=d, tiled=True)]
    all_gather x4, waiting for transfers between devices: 86.5 us -> 38.4 us  [per_device(): lax.all_gather(s, 'inner', axis=d, tiled=True)]
    all_gather x8 -> x0, blocking collectives: 35.7 us -> none  [the longest x1 4.68 us: per_device(): lax.all_gather(s_fc2_bias, 'inner', axis=0, tiled=True)]
    concatenate x0 -> x11, local copies, waits for them, and re-layouts: none -> 30.9 us  [the longest x10 30.9 us: tensor_sum(): return jnp.concatenate([first, second], axis=1)]
    select_n x0 -> x4, other arithmetic: none -> 21.4 us  [the longest x2 10.9 us: tensor_sum(): second = jnp.where(low_bit == 0, back, total)]
    psum x1, blocking collectives: 18.8 us -> 35.8 us  [per_device(): small = lax.psum(small, ('outer', 'inner'))]
  transfers between devices with their start and end apart: 13 -> 21, of which waited for: 9 -> 12; matrix products, arithmetic and copies ran while one was open for 14% -> 22% of each run, Pallas kernels for 0% -> 0%
where the time goes in v1:
time: 898 us; the launch traced here: 888 us
  waiting for transfers between devices  521 us (58%)
  local copies, waits for them, and re-layouts  113 us (13%)
  other arithmetic  99.2 us (11%)
  matrix products  93.9 us (10%)
  blocking collectives  35.8 us (4%)
  between operations  15.2 us (2%)
  starting transfers between devices  9.74 us (1%)
    psum x1, waiting for transfers between devices, per_device(): shares = lax.psum(shares, 'outer')  225 us
    ppermute x4, waiting for transfers between devices, tensor_sum(): total = part + lax.ppermute(part, 'tensor', far)  196 us
    reduce_scatter x4, waiting for transfers between devices, per_device(): lax.psum_scatter(g, 'inner', scatter_dimension=d, tiled=True)  49 us
    all_gather x4, waiting for transfers between devices, per_device(): lax.all_gather(s, 'inner', axis=d, tiled=True)  38.4 us
    unnamed x121, local copies, waits for them, and re-layouts  35.9 us
    psum x1, blocking collectives, per_device(): small = lax.psum(small, ('outer', 'inner'))  35.8 us
    concatenate x10, local copies, waits for them, and re-layouts, tensor_sum(): return jnp.concatenate([first, second], axis=1)  30.9 us
    dot_general x6, matrix products, right_contract(): lax.dot_general(left, right, (((1,), (1,)), ((), ())), preferred_element_...  25.1 us
  transfers between devices with their start and end apart: 21, of which 12 were waited for; matrix products, arithmetic and copies ran while one was open for 22% of the time, Pallas kernels for 0%

profile of v1, /device:TPU:0, one launch (start us, length us, event | category | flops | bytes accessed | tf_op | source)
XLA Modules:
  0.0 887.5 jit_solution(4057266465318198035)
XLA Ops:
  51.0 7.1 fusion.19
  74.8 51.9 %collective-permute-done.1 = f32[1154,512]{1,0:T(8,128)S(1)} collective-permute-done((f32[1154,512]{1,0:T(8,128)S(1)}, f32[1154,512]{1,0:T(8,128)S(1)}, u32[]{:S(2)}, u32[]{:S(2)}) %collective-permute-start.1) | collective-permute-done | bytes 2363424 | tf_op jit(solution)/shard_map/ppermute | solution.py:72
  128.7 4.6 copy_convert_fusion
  133.3 5.1 reshape.500
  138.4 4.7 convert_multiply_fusion
  143.1 5.0 reshape.496
  148.1 5.3 broadcast_select_fusion.7
  160.1 6.3 fusion.59
  169.6 4.8 add_convert_fusion.2
  174.5 4.7 multiply_convert_fusion.1
  184.9 4.6 fusion.65
  205.6 48.0 %collective-permute-done.7 = f32[1154,512]{1,0:T(8,128)S(1)} collective-permute-done((f32[1154,512]{1,0:T(8,128)S(1)}, f32[1154,512]{1,0:T(8,128)S(1)}, u32[]{:S(2)}, u32[]{:S(2)}) %collective-permute-start.7) | collective-permute-done | bytes 2363424 | tf_op jit(solution)/shard_map/ppermute | solution.py:72
  255.6 4.9 fusion.23
  260.6 43.5 %collective-permute-done.4 = f32[1154,512]{1,0:T(8,128)} collective-permute-done((f32[1154,512]{1,0:T(8,128)}, f32[1154,512]{1,0:T(8,128)}, u32[]{:S(2)}, u32[]{:S(2)}) %collective-permute-start.4) | collective-permute-done | bytes 2363424 | tf_op jit(solution)/shard_map/ppermute | solution.py:72
  308.5 5.2 broadcast_select_fusion.2
  328.8 7.9 convolution_convert_fusion
  338.1 6.7 convert_reduce_fusion.2
  346.8 5.3 broadcast_select_fusion.5
  358.7 9.4 %fusion.58 = (bf16[2,577,1024]{2,1,0:T(8,128)(2,1)}, f32[2,577,1024]{2,1,0:T(8,128)}, bf16[2,577,1024]{2,1,0:T(8,128)(2,1)}, f32[1024]{0:T(1024)S(1)}) fusion(f32[2,577]{1,0:T(2,128)S(1)} %negate_multiply_fusion.1, f32[2,577]{1,0:T(2,128)S(1)} %get-tuple-element.77, f32[2,577,1024]{2,1,0:T(8,128)} %get-tuple-element.55, ...), kind=kLoop, calls=%fused_computation.136 | loop fusion | flops 18906112 | bytes 26028072 | tf_op jit(solution)/shard_map/convert_element_type | solution.py:148
  375.2 6.1 multiply_reduce_fusion
  381.3 9.2 %multiply_convert_fusion = bf16[2,4,577,577]{2,3,1,0:T(8,128)(2,1)} fusion(f32[2,4,577,577]{2,3,1,0:T(8,128)S(1)} %get-tuple-element.84, f32[2,4,577,577]{2,3,1,0:T(8,128)} %copy-done.2, f32[2,4,577]{2,1,0:T(4,128)S(1)} %get-tuple-element.83, f32[2,4,577]{2,1,0:T(4,128)S(1)} %log_add_fusion), kind=kLoop, calls=%fused_computation | loop fusion | flops 13317160 | bytes 26671248 | tf_op jit(solution)/shard_map/convert_element_type | solution.py:158
  390.6 4.6 fusion.21
  404.0 5.7 fusion.12
  412.7 46.1 %reduce-scatter.5.cloned.1.call-done = f32[512,3,256]{2,0,1:T(8,128)} async-done(((f32[1024,3,256]{2,0,1:T(8,128)}), f32[512,3,256]{2,0,1:T(8,128)}) %reduce-scatter.5.cloned.1.call-update) | async-done | bytes 1572880 | tf_op jit(solution)/shard_map/reduce_scatter | solution.py:206
  458.9 225.3 %all-reduce.3.cloned.1.call-done = (f32[512,3,256]{2,0,1:T(8,128)}, f32[256,512]{1,0:T(8,128)}, f32[512,1024]{1,0:T(8,128)}, f32[1024,512]{1,0:T(8,128)}) async-done(((f32[512,3,256]{2,0,1:T(8,128)}, f32[256,512]{1,0:T(8,128)}, f32[512,1024]{1,0:T(8,128)}, f32[1024,512]{1,0:T(8,128)}), (f32[512,3,256]{2,0,1:T(8,128)}, f32[256,512]{1,0:T(8,128)}, f32[512,1024]{1,0:T(8,128)}, ...) | async-done | bytes 6291472 | tf_op jit(solution)/shard_map/psum | solution.py:209
  688.0 4.8 collective-permute-done.9
  699.1 52.2 %collective-permute-done.10 = f32[1154,512]{1,0:T(8,128)} collective-permute-done((f32[1154,512]{1,0:T(8,128)}, f32[1154,512]{1,0:T(8,128)}, u32[]{:S(2)}, u32[]{:S(2)}) %collective-permute-start.10) | collective-permute-done | bytes 2363424 | tf_op jit(solution)/shard_map/ppermute | solution.py:72
  755.8 5.5 copy.97
  764.7 5.7 broadcast_select_fusion
  788.9 35.8 %psum.35 = f32[7680]{0:T(1024)S(1)} all-reduce(f32[7680]{0:T(1024)S(1)} %constant_dynamic-update-slice_fusion.8), channel_id=1, replica_groups=mesh['outer'=4,'inner'=2,'tensor'=4] {'outer','inner'}, use_global_device_ids=true, to_apply=%region_20.21 | all-reduce | flops 7680 | bytes 61440 | tf_op jit(solution)/shard_map/psum | solution.py:195
  825.2 5.7 copy.98
  831.6 38.3 %all-gather.11.cloned.1.call-done = f32[1024,1024]{1,0:T(8,128)} async-done(((f32[1024,512]{1,0:T(8,128)}), f32[1024,1024]{1,0:T(8,128)}) %all-gather.11.cloned.1.call-update) | async-done | bytes 4194320 | tf_op jit(solution)/shard_map/all_gather | solution.py:211
  (253 shorter events, 192.3 us)
Async XLA Ops:
  7.2 167.2 %copy-start = (bf16[1024,1024]{1,0:T(8,128)(2,1)S(1)}, bf16[1024,1024]{1,0:T(8,128)(2,1)}, u32[]{:S(2)}) copy-start(bf16[1024,1024]{1,0:T(8,128)(2,1)} %param.24) | copy-start | bytes 6291460
  7.2 402.6 %reduce-scatter.9.cloned.1.call-start = ((), (), s32[]{:S(2)}) async-start(), calls=%async_computation.8 | async-start | bytes 6291456 | tf_op jit(solution)/shard_map/reduce_scatter | solution.py:206
  30.6 7.7 copy-start.35
  32.7 8.9 %copy-start.10 = (f32[2,577,4,64]{1,3,2,0:T(8,128)}, f32[2,577,4,64]{1,3,2,0:T(8,128)S(1)}, u32[]{:S(2)}) copy-start(f32[2,577,4,64]{1,3,2,0:T(8,128)S(1)} %copy.80) | copy-start | bytes 3545092
  59.7 10.0 %copy-start.18 = (bf16[256,1024]{1,0:T(8,128)(2,1)S(1)}, bf16[256,1024]{1,0:T(8,128)(2,1)}, u32[]{:S(2)}) copy-start(bf16[256,1024]{1,0:T(8,128)(2,1)} %param.20) | copy-start | bytes 1572868
  64.7 5.0 collective-permute-start
  71.9 54.8 %collective-permute-start.1 = (f32[1154,512]{1,0:T(8,128)S(1)}, f32[1154,512]{1,0:T(8,128)S(1)}, u32[]{:S(2)}, u32[]{:S(2)}) collective-permute-start(f32[1154,512]{1,0:T(8,128)S(1)} %convolution_add_fusion.1), channel_id=1, source_target_pairs={{0,2},{1,3},{2,0},{3,1},{4,6},{5,7},{6,4},{7,5},{8,10},{9,11},{10,... | collective-permute-start | bytes 7090184 | tf_op jit(solution)/shard_map/ppermute | solution.py:72
  128.7 19.5 %collective-permute-start.2 = (f32[1154,512]{1,0:T(8,128)}, f32[1154,512]{1,0:T(8,128)}, u32[]{:S(2)}, u32[]{:S(2)}) collective-permute-start(f32[1154,512]{1,0:T(8,128)} %add.226), channel_id=1, source_target_pairs={{0,1},{1,0},{2,3},{3,2},{4,5},{5,4},{6,7},{7,6},{8,9},{9,8},{10,11... | collective-permute-start | bytes 7090184 | tf_op jit(solution)/shard_map/ppermute | solution.py:73
  169.6 9.6 %slice-start.4 = ((s8[4751360]{0:T(1024)(128)(4,1)}), s8[4194304]{0:T(1024)(128)(4,1)S(1)}, s32[]{:S(2)}) async-start(s8[4751360]{0:T(1024)(128)(4,1)} %bitcast.70), calls=%async_computation.17 | async-start | bytes 8388608
  189.5 220.3 %reduce-scatter.11.cloned.1.call-start = ((), (), s32[]{:S(2)}) async-start(), calls=%async_computation.10 | async-start | bytes 6291456 | tf_op jit(solution)/shard_map/reduce_scatter | solution.py:206
  192.8 4.8 collective-permute-start.6
  194.8 6.2 collective-permute-start.3
  197.6 58.0 %slice-start.6 = ((s8[4751360]{0:T(1024)(128)(4,1)}), s8[4194304]{0:T(1024)(128)(4,1)S(1)}, s32[]{:S(2)}) async-start(s8[4751360]{0:T(1024)(128)(4,1)} %bitcast.72), calls=%async_computation.19 | async-start | bytes 8388608
  199.1 56.5 %slice-start.7 = ((s8[4751360]{0:T(1024)(128)(4,1)}), s8[557056]{0:T(1024)(128)(4,1)S(1)}, s32[]{:S(2)}) async-start(s8[4751360]{0:T(1024)(128)(4,1)} %bitcast.72), calls=%async_computation.20 | async-start | bytes 1114112
  199.1 54.5 %collective-permute-start.7 = (f32[1154,512]{1,0:T(8,128)S(1)}, f32[1154,512]{1,0:T(8,128)S(1)}, u32[]{:S(2)}, u32[]{:S(2)}) collective-permute-start(f32[1154,512]{1,0:T(8,128)S(1)} %convolution_add_fusion.3), channel_id=1, source_target_pairs={{0,2},{1,3},{2,0},{3,1},{4,6},{5,7},{6,4},{7,5},{8,10},{9,11},{10,... | collective-permute-start | bytes 7090184 | tf_op jit(solution)/shard_map/ppermute | solution.py:72
  203.9 100.2 %collective-permute-start.4 = (f32[1154,512]{1,0:T(8,128)}, f32[1154,512]{1,0:T(8,128)}, u32[]{:S(2)}, u32[]{:S(2)}) collective-permute-start(f32[1154,512]{1,0:T(8,128)} %convolution_add_fusion.4), channel_id=1, source_target_pairs={{0,2},{1,3},{2,0},{3,1},{4,6},{5,7},{6,4},{7,5},{8,10},{9,11},{10,... | collective-permute-start | bytes 7090184 | tf_op jit(solution)/shard_map/ppermute | solution.py:72
  255.6 52.9 %collective-permute-start.8 = (f32[1154,512]{1,0:T(8,128)}, f32[1154,512]{1,0:T(8,128)}, u32[]{:S(2)}, u32[]{:S(2)}) collective-permute-start(f32[1154,512]{1,0:T(8,128)} %add.247), channel_id=1, source_target_pairs={{0,1},{1,0},{2,3},{3,2},{4,5},{5,4},{6,7},{7,6},{8,9},{9,8},{10,11... | collective-permute-start | bytes 7090184 | tf_op jit(solution)/shard_map/ppermute | solution.py:73
  260.5 152.1 %reduce-scatter.7.cloned.1.call-start = ((), (), s32[]{:S(2)}) async-start(), calls=%async_computation.6 | async-start | bytes 1572864 | tf_op jit(solution)/shard_map/reduce_scatter | solution.py:206
  308.5 38.3 %collective-permute-start.5 = (f32[1154,512]{1,0:T(8,128)}, f32[1154,512]{1,0:T(8,128)}, u32[]{:S(2)}, u32[]{:S(2)}) collective-permute-start(f32[1154,512]{1,0:T(8,128)} %add.241), channel_id=1, source_target_pairs={{0,1},{1,0},{2,3},{3,2},{4,5},{5,4},{6,7},{7,6},{8,9},{9,8},{10,11... | collective-permute-start | bytes 7090184 | tf_op jit(solution)/shard_map/ppermute | solution.py:73
  381.3 9.3 %copy-start.11 = (f32[2,577,4,64]{1,3,2,0:T(8,128)S(1)}, f32[2,577,4,64]{1,3,2,0:T(8,128)}, u32[]{:S(2)}) copy-start(f32[2,577,4,64]{1,3,2,0:T(8,128)} %copy-done.10) | copy-start | bytes 3545092
  381.3 9.3 %copy-start.28 = (f32[4,64]{1,0:T(4,128)S(1)}, f32[4,64]{1,0:T(4,128)}, u32[]{:S(2)}) copy-start(f32[4,64]{1,0:T(4,128)} %copy-done.27) | copy-start | bytes 3076
  390.5 68.3 %reduce-scatter.5.cloned.1.call-start = ((), (), s32[]{:S(2)}) async-start(), calls=%async_computation.4 | async-start | bytes 4718592 | tf_op jit(solution)/shard_map/reduce_scatter | solution.py:206
  409.7 274.5 %all-reduce.3.cloned.1.call-start = ((), (), s32[]{:S(2)}) async-start(), calls=%async_computation.12 | async-start | bytes 12582912 | tf_op jit(solution)/shard_map/psum | solution.py:209
  458.8 372.7 %all-gather.7.cloned.1.call-start = ((), (), s32[]{:S(2)}) async-start(), calls=%async_computation.7 | async-start | bytes 1572864 | tf_op jit(solution)/shard_map/all_gather | solution.py:211
  684.2 147.3 %all-gather.5.cloned.1.call-start = ((), (), s32[]{:S(2)}) async-start(), calls=%async_computation.5 | async-start | bytes 4718592 | tf_op jit(solution)/shard_map/all_gather | solution.py:211
  687.9 4.9 collective-permute-start.9
  688.0 143.6 %all-gather.9.cloned.1.call-start = ((), (), s32[]{:S(2)}) async-start(), calls=%async_computation.9 | async-start | bytes 6291456 | tf_op jit(solution)/shard_map/all_gather | solution.py:211
  697.3 54.0 %collective-permute-start.10 = (f32[1154,512]{1,0:T(8,128)}, f32[1154,512]{1,0:T(8,128)}, u32[]{:S(2)}, u32[]{:S(2)}) collective-permute-start(f32[1154,512]{1,0:T(8,128)} %convolution_add_fusion.2), channel_id=1, source_target_pairs={{0,2},{1,3},{2,0},{3,1},{4,6},{5,7},{6,4},{7,5},{8,10},{9,11},{10,... | collective-permute-start | bytes 7090184 | tf_op jit(solution)/shard_map/ppermute | solution.py:72
  698.8 171.1 %all-gather.11.cloned.1.call-start = ((), (), s32[]{:S(2)}) async-start(), calls=%async_computation.11 | async-start | bytes 6291456 | tf_op jit(solution)/shard_map/all_gather | solution.py:211
  755.6 9.0 %collective-permute-start.11 = (f32[1154,512]{1,0:T(8,128)}, f32[1154,512]{1,0:T(8,128)}, u32[]{:S(2)}, u32[]{:S(2)}) collective-permute-start(f32[1154,512]{1,0:T(8,128)} %add.251), channel_id=1, source_target_pairs={{0,1},{1,0},{2,3},{3,2},{4,5},{5,4},{6,7},{7,6},{8,9},{9,8},{10,11... | collective-permute-start | bytes 7090184 | tf_op jit(solution)/shard_map/ppermute | solution.py:73
  776.9 8.7 slice-start.2
  831.5 42.3 %copy-start.17 = (f32[256,1024]{1,0:T(8,128)S(1)}, f32[256,1024]{1,0:T(8,128)}, u32[]{:S(2)}) copy-start(f32[256,1024]{1,0:T(8,128)} %all-gather.7.cloned.1.call-done) | copy-start | bytes 3145732
  (40 other events, 166.6 us)
Sparse Core Ops, SparseCore 0:
  189.6 55.9 reduce-scatter.8
  260.6 55.9 reduce-scatter.10
  390.6 21.9 reduce-scatter.6
  415.3 43.4 reduce-scatter.4
  461.3 222.9 all-reduce.2
  685.6 20.1 all-gather.6
  707.4 44.8 all-gather.4
  753.9 57.5 all-gather.8
  813.0 56.8 all-gather.10
